TPU v7x, 512 devices: a whole 4x4x16 slice. The times are simulated.
512 devices in a mesh: outer: 32 (over z, x_hi), inner: 16 (over x_lo, y, core).
Axes of the slice: x: 4 (x_hi: 2, x_lo: 2; x = x_hi * 2 + x_lo), y: 4, z: 16, core: 2. Of those that a mesh axis runs over, the one named last changes fastest.
Arguments:
- queries: bfloat16 [16384, 128], P('inner'), may hold values from -150 to 150
- key_rows: bfloat16 [131072, 128], P(('outer', 'inner')), may hold values from -4.5 to 4.5
- value_rows: bfloat16 [131072, 128], P(('outer', 'inner')), may hold values from -6 to 6
Outputs:
- attended: bfloat16 [16384, 128], P('inner')
All inputs are finite; a program needn't handle non-finite values.
Results may differ from a plain program's by a relative error of at most 0.015.
Values may be sent and summed in bfloat16 or wider, within the bound.
No kernel may reach another device: no remote copies, remote signals or barrier semaphores. Data moves between devices by JAX's collectives and lax.ppermute only.
A program may use at most 64 MiB of HBM per device.

v0:
```python
import math
import jax
import jax.numpy as jnp
from jax import lax
from jax.sharding import PartitionSpec as P


def merged(part, axis, combine):
    gathered = jax.tree.map(lambda a: lax.all_gather(a, axis), part)

    def take(source):
        return jax.tree.map(lambda a: lax.dynamic_index_in_dim(a, source, 0, False), gathered)

    return lax.fori_loop(
        1, lax.axis_size(axis), lambda source, state: combine(state, take(source)), take(0)
    )


def combine_partial(left, right):
    left_sum, left_peak, left_total = left
    right_sum, right_peak, right_total = right
    joint_peak = jnp.maximum(left_peak, right_peak)
    left_factor = jnp.exp(left_peak - joint_peak)
    right_factor = jnp.exp(right_peak - joint_peak)
    joint_sum = left_sum * left_factor[:, None] + right_sum * right_factor[:, None]
    joint_total = left_total * left_factor + right_total * right_factor
    return (joint_sum, joint_peak, joint_total)


def on_device(queries, key_rows, value_rows):
    query_count, head_size = queries.shape
    score_scale = 1.0 / math.sqrt(head_size)

    def advance(running, tiles):
        weighted, row_peak, row_total = running
        key_tile, value_tile = tiles
        scores = (
            lax.dot_general(
                queries, key_tile, (((1,), (1,)), ((), ())), preferred_element_type=jnp.float32
            )
            * score_scale
        )
        new_peak = jnp.maximum(row_peak, jnp.max(scores, axis=1))
        rescale = jnp.exp(row_peak - new_peak)
        probs = jnp.exp(scores - new_peak[:, None])
        new_total = row_total * rescale + jnp.sum(probs, axis=1)
        new_weighted = weighted * rescale[:, None] + jnp.dot(
            probs.astype(jnp.bfloat16), value_tile, preferred_element_type=jnp.float32
        )
        return ((new_weighted, new_peak, new_total), None)

    start_state = (
        jnp.zeros((query_count, head_size), jnp.float32),
        jnp.full((query_count,), -1e30, jnp.float32),
        jnp.zeros((query_count,), jnp.float32),
    )
    key_part = lax.all_gather(key_rows, "inner", axis=0, tiled=True)
    value_part = lax.all_gather(value_rows, "inner", axis=0, tiled=True)
    row_count = key_part.shape[0]
    block_rows = math.gcd(row_count, 256)
    key_tiles = key_part.reshape(row_count // block_rows, block_rows, head_size)
    value_tiles = value_part.reshape(row_count // block_rows, block_rows, head_size)
    result, unused = lax.scan(advance, start_state, (key_tiles, value_tiles))
    weighted, row_peak, row_total = result
    joint_sum, joint_peak, joint_total = merged(
        (weighted, row_peak, row_total), "outer", combine_partial
    )
    attended = (joint_sum / joint_total[:, None]).astype(jnp.bfloat16)
    return attended


def solution(mesh):
    return jax.shard_map(
        on_device,
        mesh=mesh,
        in_specs=(P("inner", None), P(("outer", "inner"), None), P(("outer", "inner"), None)),
        out_specs=P("inner", None),
        check_vma=False,
    )
```

profile of v0, /device:TPU:1, one launch (start us, length us, event | category | flops | bytes accessed | tf_op | source)
XLA Modules:
  0.0 469.2 jit_solution(17336920860989906849)
XLA Ops:
  8.1 46.9 %all-gather.7.cloned.1.call-done = bf16[4096,128]{1,0:T(8,128)(2,1)} async-done(((bf16[256,128]{1,0:T(8,128)(2,1)}), bf16[4096,128]{1,0:T(8,128)(2,1)}) %all-gather.7.cloned.1.call-update) | async-done | bytes 1048592 | tf_op jit(solution)/shard_map/all_gather | solution.py:57
  55.0 42.1 %all-gather.9.cloned.1.call-done = bf16[4096,128]{1,0:T(8,128)(2,1)} async-done(((bf16[256,128]{1,0:T(8,128)(2,1)}), bf16[4096,128]{1,0:T(8,128)(2,1)}) %all-gather.9.cloned.1.call-update) | async-done | bytes 1048592 | tf_op jit(solution)/shard_map/all_gather | solution.py:58
  97.1 46.3 %while.35 = (s32[]{:T(128)}, f32[1024,128]{1,0:T(8,128)S(1)}, f32[1024]{0:T(1024)S(1)}, f32[1024]{0:T(1024)S(1)}, bf16[16,256,128]{2,1,0:T(8,128)(2,1)}, /*index...) while((s32[]{:T(128)}, f32[1024,128]{1,0:T(8,128)S(1)}, ...), condition=%wide.region_3.4_spmd.clone, body=%wide.region_0.3_spmd.clone.sunk | while | flops 136188928 | bytes 4653177 | solution.py:63
  98.6 1.4 convolution_add_fusion.2
  100.0 1.3 fusion.25
  101.5 1.4 convolution_add_fusion.2
  102.9 1.3 fusion.25
  104.4 1.4 convolution_add_fusion.2
  105.8 1.3 fusion.25
  107.3 1.4 convolution_add_fusion.2
  108.7 1.3 fusion.25
  110.2 1.4 convolution_add_fusion.2
  111.6 1.3 fusion.25
  113.1 1.4 convolution_add_fusion.2
  114.5 1.3 fusion.25
  116.0 1.4 convolution_add_fusion.2
  117.4 1.3 fusion.25
  118.9 1.4 convolution_add_fusion.2
  121.8 1.4 convolution_add_fusion.2
  124.7 1.4 convolution_add_fusion.2
  126.1 1.3 fusion.25
  127.6 1.4 convolution_add_fusion.2
  129.0 1.3 fusion.25
  130.5 1.4 convolution_add_fusion.2
  131.9 1.3 fusion.25
  133.4 1.4 convolution_add_fusion.2
  136.3 1.4 convolution_add_fusion.2
  139.2 1.4 convolution_add_fusion.2
  142.1 1.4 convolution_add_fusion.2
  144.3 63.4 %all-gather.2 = f32[32768]{0:T(1024)S(1)} all-gather(f32[1024]{0:T(1024)S(1)} %get-tuple-element.223), channel_id=4, replica_groups=mesh['outer'=32,'inner'=16] {'outer'}, dimensions={0}, use_global_device_ids=true | all-gather | bytes 135168 | tf_op jit(solution)/shard_map/all_gather | solution.py:9
  207.7 58.3 %all-gather.1 = f32[32768]{0:T(1024)S(1)} all-gather(f32[1024]{0:T(1024)S(1)} %get-tuple-element.222), channel_id=3, replica_groups=mesh['outer'=32,'inner'=16] {'outer'}, dimensions={0}, use_global_device_ids=true | all-gather | bytes 135168 | tf_op jit(solution)/shard_map/all_gather | solution.py:9
  266.1 146.1 %all-gather.11.cloned.1.call-done = f32[32768,128]{1,0:T(8,128)} async-done(((f32[1024,128]{1,0:T(8,128)}), f32[32768,128]{1,0:T(8,128)}) %all-gather.11.cloned.1.call-update) | async-done | bytes 16777232 | tf_op jit(solution)/shard_map/all_gather | solution.py:9
  413.2 48.5 %while.34 = (s32[]{:T(128)}, f32[1024,128]{1,0:T(8,128)S(1)}, f32[1024]{0:T(1024)S(1)}, f32[1024]{0:T(1024)S(1)}, f32[32,1024]{1,0:T(8,128)S(1)}, /*index=5*/f32...) while((s32[]{:T(128)}, f32[1024,128]{1,0:T(8,128)S(1)}, ...), condition=%wide.region_5.6_spmd, body=%wide.region_4.5_spmd.sunk | while | flops 399365 | bytes 1630351 | solution.py:14
  413.3 1.5 fusion.21
  414.8 1.5 fusion.21
  416.4 1.5 fusion.21
  418.0 1.5 fusion.21
  419.5 1.5 fusion.21
  421.1 1.5 fusion.21
  422.7 1.5 fusion.21
  424.2 1.5 fusion.21
  425.8 1.5 fusion.21
  427.4 1.5 fusion.21
  428.9 1.5 fusion.21
  430.5 1.5 fusion.21
  432.0 1.5 fusion.21
  433.6 1.5 fusion.21
  435.2 1.5 fusion.21
  436.7 1.5 fusion.21
  438.3 1.5 fusion.21
  439.9 1.5 fusion.21
  441.4 1.5 fusion.21
  443.0 1.5 fusion.21
  444.6 1.5 fusion.21
  446.1 1.5 fusion.21
  447.7 1.5 fusion.21
  449.3 1.5 fusion.21
  450.8 1.5 fusion.21
  452.4 1.5 fusion.21
  453.9 1.5 fusion.21
  455.5 1.5 fusion.21
  457.1 1.5 fusion.21
  458.6 1.5 fusion.21
  460.2 1.5 fusion.21
  (149 shorter events, 16.0 us)
Async XLA Ops:
  6.5 48.5 %all-gather.7.cloned.1.call-start = ((), (), s32[]{:S(2)}) async-start(), calls=%async_computation | async-start | bytes 1114112 | tf_op jit(solution)/shard_map/all_gather | solution.py:57
  7.3 89.8 %all-gather.9.cloned.1.call-start = ((), (), s32[]{:S(2)}) async-start(), calls=%async_computation.1 | async-start | bytes 1114112 | tf_op jit(solution)/shard_map/all_gather | solution.py:58
  8.0 404.1 %all-gather.11.cloned.1.call-start = ((), (), s32[]{:S(2)}) async-start(), calls=%async_computation.2 | async-start | bytes 17301504 | tf_op jit(solution)/shard_map/all_gather | solution.py:9
  143.4 0.8 copy-start
Sparse Core Ops, SparseCore 0:
  9.5 45.4 all-gather.6
  57.2 39.9 all-gather.8
  144.4 267.7 all-gather.10
where the time goes:
time: 472 us; the launch traced here: 469 us
  waiting for transfers between devices  236 us (50%)
  blocking collectives  122 us (26%)
  other arithmetic  50.8 us (11%)
  matrix products  42.5 us (9%)
  between operations  13.2 us (3%)
    all_gather x1, waiting for transfers between devices, merged(): gathered = jax.tree.map(lambda a: lax.all_gather(a, axis), part)  146 us
    all_gather x2, blocking collectives, merged(): gathered = jax.tree.map(lambda a: lax.all_gather(a, axis), part)  122 us
    all_gather x1, waiting for transfers between devices, on_device(): key_part = lax.all_gather(key_rows, 'inner', axis=0, tiled=True)  46.9 us
    add x31, other arithmetic, combine_partial(): left_sum * left_factor[:, None] + right_sum * right_factor[:, None]  46.5 us
    all_gather x1, waiting for transfers between devices, on_device(): value_part = lax.all_gather(value_rows, 'inner', axis=0, tiled=True)  42.1 us
    dot_general x16, matrix products, advance(): jnp.dot(probs.astype(jnp.bfloat16), value_tile, preferred_element_type=jn...  21.7 us
    dot_general x16, matrix products, advance(): lax.dot_general(queries, key_tile, (((1,), (1,)), ((), ())), preferred_el...  20.8 us
  transfers between devices with their start and end apart: 3, of which 3 were waited for; matrix products, arithmetic and copies ran while one was open for 0% of the time, Pallas kernels for 0%

commit v1 on v0

--- a/solution.py
+++ b/solution.py
@@ -3,6 +3,15 @@
 import jax.numpy as jnp
 from jax import lax
 from jax.sharding import PartitionSpec as P
+from jax.lax import all_to_all, axis_size
+
+
+def signs_replace(x0):
+    front = jnp.concatenate(
+        all_to_all(jnp.stack([x0] * axis_size("inner")), "inner", split_axis=0, concat_axis=0),
+        axis=0,
+    )
+    return front
 
 
 def merged(part, axis, combine):
@@ -54,7 +63,7 @@
         jnp.full((query_count,), -1e30, jnp.float32),
         jnp.zeros((query_count,), jnp.float32),
     )
-    key_part = lax.all_gather(key_rows, "inner", axis=0, tiled=True)
+    key_part = signs_replace(key_rows)
     value_part = lax.all_gather(value_rows, "inner", axis=0, tiled=True)
     row_count = key_part.shape[0]
     block_rows = math.gcd(row_count, 256)

time: 472 us -> 430 us (0.911)
  waiting for transfers between devices: 236 us -> 180 us
  starting transfers between devices: 0.08 us -> 10.3 us
    all_gather x1 -> x0, waiting for transfers between devices: 46.9 us -> none  [on_device(): key_part = lax.all_gather(key_rows, 'inner', axis=0, tiled=True)]
    all_gather x1, waiting for transfers between devices: 42.1 us -> 19.5 us  [on_device(): value_part = lax.all_gather(value_rows, 'inner', axis=0, tiled=True)]
    all_to_all x0 -> x1, waiting for transfers between devices: none -> 15.7 us  [signs_replace(): all_to_all(jnp.stack([x0] * axis_size('inner')), 'inner', split_axis=0, c...]
    all_to_all x0 -> x1, starting transfers between devices: none -> 10.3 us  [signs_replace(): all_to_all(jnp.stack([x0] * axis_size('inner')), 'inner', split_axis=0, c...]
where the time goes in v1:
time: 430 us; the launch traced here: 427 us
  waiting for transfers between devices  180 us (42%)
  blocking collectives  123 us (29%)
  other arithmetic  50.8 us (12%)
  matrix products  41.8 us (10%)
  between operations  13.5 us (3%)
  starting transfers between devices  10.3 us (2%)
  local copies, waits for them, and re-layouts  4.5 us (1%)
    all_gather x1, waiting for transfers between devices, merged(): gathered = jax.tree.map(lambda a: lax.all_gather(a, axis), part)  145 us
    all_gather x2, blocking collectives, merged(): gathered = jax.tree.map(lambda a: lax.all_gather(a, axis), part)  123 us
    add x31, other arithmetic, combine_partial(): left_sum * left_factor[:, None] + right_sum * right_factor[:, None]  46.5 us
    dot_general x16, matrix products, advance(): jnp.dot(probs.astype(jnp.bfloat16), value_tile, preferred_element_type=jn...  21.7 us
    dot_general x16, matrix products, advance(): lax.dot_general(queries, key_tile, (((1,), (1,)), ((), ())), preferred_el...  20.1 us
    all_gather x1, waiting for transfers between devices, on_device(): value_part = lax.all_gather(value_rows, 'inner', axis=0, tiled=True)  19.5 us
    all_to_all x1, waiting for transfers between devices, signs_replace(): all_to_all(jnp.stack([x0] * axis_size('inner')), 'inner', split_axis=0, c...  15.7 us
    all_to_all x1, starting transfers between devices, signs_replace(): all_to_all(jnp.stack([x0] * axis_size('inner')), 'inner', split_axis=0, c...  10.3 us
  transfers between devices with their start and end apart: 3, of which 3 were waited for; matrix products, arithmetic and copies ran while one was open for 0% of the time, Pallas kernels for 0%

profile of v1, /device:TPU:1, one launch (start us, length us, event | category | flops | bytes accessed | tf_op | source)
XLA Modules:
  0.0 426.6 jit_solution(2505914010441884048)
XLA Ops:
  7.3 2.1 stack.2
  9.3 10.3 %all-to-all-start = ((bf16[16,256,128]{2,1,0:T(8,128)(2,1)}), bf16[16,256,128]{2,1,0:T(8,128)(2,1)S(1)}, u32[]{:S(2)}, u32[]{:S(2)}) async-start(bf16[16,256,128]{2,1,0:T(8,128)(2,1)} %stack.2), calls=%async_computation | async-start | bytes 2097152 | tf_op jit(solution)/shard_map/all_to_all | solution.py:11
  19.7 15.7 %all-to-all-done = bf16[16,256,128]{2,1,0:T(8,128)(2,1)S(1)} async-done(((bf16[16,256,128]{2,1,0:T(8,128)(2,1)}), bf16[16,256,128]{2,1,0:T(8,128)(2,1)S(1)}, u32[]{:S(2)}, u32[]{:S(2)}) %all-to-all-start) | async-done | bytes 1048608 | tf_op jit(solution)/shard_map/all_to_all | solution.py:11
  35.4 19.5 %all-gather.6.cloned.1.call-done = bf16[4096,128]{1,0:T(8,128)(2,1)} async-done(((bf16[256,128]{1,0:T(8,128)(2,1)}), bf16[4096,128]{1,0:T(8,128)(2,1)}) %all-gather.6.cloned.1.call-update) | async-done | bytes 1048592 | tf_op jit(solution)/shard_map/all_gather | solution.py:67
  54.9 45.7 %while.35 = (s32[]{:T(128)}, f32[1024,128]{1,0:T(8,128)S(1)}, f32[1024]{0:T(1024)S(1)}, f32[1024]{0:T(1024)S(1)}, bf16[16,256,128]{2,1,0:T(8,128)(2,1)S(1)}, /*i...) while((s32[]{:T(128)}, f32[1024,128]{1,0:T(8,128)S(1)}, ...), condition=%wide.region_3.4_spmd.clone, body=%wide.region_0.3_spmd.clone.sunk | while | flops 136188928 | bytes 4653177 | solution.py:72
  56.4 1.4 convolution_add_fusion.2
  57.8 1.3 fusion.25
  59.2 1.4 convolution_add_fusion.2
  60.6 1.3 fusion.25
  62.1 1.4 convolution_add_fusion.2
  63.5 1.3 fusion.25
  64.9 1.4 convolution_add_fusion.2
  66.3 1.3 fusion.25
  67.8 1.4 convolution_add_fusion.2
  69.2 1.3 fusion.25
  70.6 1.4 convolution_add_fusion.2
  73.5 1.4 convolution_add_fusion.2
  76.4 1.4 convolution_add_fusion.2
  77.7 1.3 fusion.25
  79.2 1.4 convolution_add_fusion.2
  80.6 1.3 fusion.25
  82.1 1.4 convolution_add_fusion.2
  83.5 1.3 fusion.25
  84.9 1.4 convolution_add_fusion.2
  87.8 1.4 convolution_add_fusion.2
  90.6 1.4 convolution_add_fusion.2
  93.5 1.4 convolution_add_fusion.2
  96.3 1.4 convolution_add_fusion.2
  99.2 1.4 convolution_add_fusion.2
  101.4 65.3 %all-gather.2 = f32[32768]{0:T(1024)S(1)} all-gather(f32[1024]{0:T(1024)S(1)} %get-tuple-element.223), channel_id=4, replica_groups=mesh['outer'=32,'inner'=16] {'outer'}, dimensions={0}, use_global_device_ids=true | all-gather | bytes 135168 | tf_op jit(solution)/shard_map/all_gather | solution.py:18
  166.8 58.0 %all-gather.1 = f32[32768]{0:T(1024)S(1)} all-gather(f32[1024]{0:T(1024)S(1)} %get-tuple-element.222), channel_id=3, replica_groups=mesh['outer'=32,'inner'=16] {'outer'}, dimensions={0}, use_global_device_ids=true | all-gather | bytes 135168 | tf_op jit(solution)/shard_map/all_gather | solution.py:18
  224.8 144.5 %all-gather.8.cloned.1.call-done = f32[32768,128]{1,0:T(8,128)} async-done(((f32[1024,128]{1,0:T(8,128)}), f32[32768,128]{1,0:T(8,128)}) %all-gather.8.cloned.1.call-update) | async-done | bytes 16777232 | tf_op jit(solution)/shard_map/all_gather | solution.py:18
  370.4 48.5 %while.34 = (s32[]{:T(128)}, f32[1024,128]{1,0:T(8,128)S(1)}, f32[1024]{0:T(1024)S(1)}, f32[1024]{0:T(1024)S(1)}, f32[32,1024]{1,0:T(8,128)S(1)}, /*index=5*/f32...) while((s32[]{:T(128)}, f32[1024,128]{1,0:T(8,128)S(1)}, ...), condition=%wide.region_5.6_spmd, body=%wide.region_4.5_spmd.sunk | while | flops 399365 | bytes 1630351 | solution.py:23
  370.4 1.5 fusion.21
  372.0 1.5 fusion.21
  373.6 1.5 fusion.21
  375.1 1.5 fusion.21
  376.7 1.5 fusion.21
  378.2 1.5 fusion.21
  379.8 1.5 fusion.21
  381.4 1.5 fusion.21
  382.9 1.5 fusion.21
  384.5 1.5 fusion.21
  386.1 1.5 fusion.21
  387.6 1.5 fusion.21
  389.2 1.5 fusion.21
  390.8 1.5 fusion.21
  392.3 1.5 fusion.21
  393.9 1.5 fusion.21
  395.5 1.5 fusion.21
  397.0 1.5 fusion.21
  398.6 1.5 fusion.21
  400.1 1.5 fusion.21
  401.7 1.5 fusion.21
  403.3 1.5 fusion.21
  404.8 1.5 fusion.21
  406.4 1.5 fusion.21
  408.0 1.5 fusion.21
  409.5 1.5 fusion.21
  411.1 1.5 fusion.21
  412.7 1.5 fusion.21
  414.2 1.5 fusion.21
  415.8 1.5 fusion.21
  417.4 1.5 fusion.21
  (149 shorter events, 17.6 us)
Async XLA Ops:
  6.5 48.4 %all-gather.6.cloned.1.call-start = ((), (), s32[]{:S(2)}) async-start(), calls=%async_computation.1 | async-start | bytes 1114112 | tf_op jit(solution)/shard_map/all_gather | solution.py:67
  9.3 26.0 %all-to-all-start = ((bf16[16,256,128]{2,1,0:T(8,128)(2,1)}), bf16[16,256,128]{2,1,0:T(8,128)(2,1)S(1)}, u32[]{:S(2)}, u32[]{:S(2)}) async-start(bf16[16,256,128]{2,1,0:T(8,128)(2,1)} %stack.2), calls=%async_computation | async-start | bytes 2097152 | tf_op jit(solution)/shard_map/all_to_all | solution.py:11
  19.6 349.7 %all-gather.8.cloned.1.call-start = ((), (), s32[]{:S(2)}) async-start(), calls=%async_computation.2 | async-start | bytes 17301504 | tf_op jit(solution)/shard_map/all_gather | solution.py:18
  100.6 0.8 copy-start
Sparse Core Ops, SparseCore 0:
  9.5 45.3 all-gather.5
  101.5 267.7 all-gather.7
